TPU v7x, 32 devices: a whole 2x2x4 slice. The times are simulated.
32 devices in a mesh: dp: 8 (over z, y), feat: 4 (over x, core).
Axes of the slice: x: 2, y: 2, z: 4, core: 2. Of those that a mesh axis runs over, the one named last changes fastest.
Arguments:
- activations: bfloat16 [16384, 2048], P('feat', 'dp'), may hold values from -6 to 6
- cotangent: bfloat16 [16384, 2048], P('feat', 'dp'), may hold values from -6 to 6
- r_mix: bfloat16 [64, 256, 256], P('feat', 'dp'), may hold values from -0.375 to 0.375
- l_mix: bfloat16 [256, 4096], P('feat', 'dp'), may hold values from -0.75 to 0.75
Outputs:
- grad_x: bfloat16 [16384, 2048], P('feat', 'dp')
- grad_r: float32 [64, 256, 256], P('feat', 'dp')
- grad_l: float32 [256, 4096], P('feat', 'dp')
All inputs are finite; a program needn't handle non-finite values.
Results may differ from a plain program's by a relative error of at most 0.0055.
Values may be sent and summed in bfloat16 or wider, within the bound.
No kernel may reach another device: no remote copies, remote signals or barrier semaphores. Data moves between devices by JAX's collectives and lax.ppermute only.
A program may use at most 64 MiB of HBM per device.

v0:
```python
import math
import jax
import jax.numpy as jnp
import numpy as np
from jax import lax
from jax.sharding import PartitionSpec as P

BLOCKS = 64
WIDTH = 256


def gelu_tanh(values):
    return jax.nn.gelu(values, approximate=True)


def slope_of(pre_act, upstream):
    _, pullback = jax.vjp(gelu_tanh, pre_act)
    return pullback(upstream.astype(jnp.float32))[0].astype(jnp.bfloat16)


def ring_of(mesh):
    row = mesh.devices[(slice(None),) + (0,) * (mesh.devices.ndim - 1)]
    size = len(row)
    try:
        spots = [tuple(d.coords) for d in row]
    except AttributeError:
        return list(range(size))
    near = [
        [j for j in range(size) if sum((abs(a - b) for a, b in zip(spots[i], spots[j]))) == 1]
        for i in range(size)
    ]
    path, seen, budget = ([0], {0}, [20000])

    def grow():
        budget[0] -= 1
        if budget[0] < 0:
            return False
        if len(path) == size:
            return 0 in near[path[-1]] or size <= 2
        here = path[-1]
        for nxt in sorted(near[here], key=lambda j: len([k for k in near[j] if k not in seen])):
            if nxt in seen:
                continue
            path.append(nxt)
            seen.add(nxt)
            if grow():
                return True
            path.pop()
            seen.discard(nxt)
        return False

    return list(path) if grow() else list(range(size))


def ring_reduce_scatter(parts, ring):
    n = len(ring)
    order = jnp.asarray(np.array(ring, np.int32))
    place = jnp.asarray(np.argsort(np.array(ring)).astype(np.int32))
    here = place[lax.axis_index("dp")]
    half = parts.shape[1] // 2
    halves = (parts[:, :half], parts[:, half:])
    forward = [(ring[p], ring[(p + 1) % n]) for p in range(n)]
    backward = [(ring[p], ring[(p - 1) % n]) for p in range(n)]
    totals = []
    for way, pairs, src in ((1, forward, halves[0]), (-1, backward, halves[1])):
        acc = None
        for step in range(n):
            owner = order[(here - way * (1 + step)) % n]
            mine = lax.dynamic_index_in_dim(src, owner, axis=0, keepdims=False)
            acc = mine if acc is None else acc + mine
            if step < n - 1:
                acc = lax.ppermute(acc, "dp", pairs)
        totals.append(acc)
    return jnp.concatenate(totals, axis=0)


def body(ring, activations, cotangent, r_mix, l_mix):
    tok_count = activations.shape[1]
    local_blocks = activations.shape[0] // WIDTH
    n_dp = lax.axis_size("dp")
    grad_scale = 1.0 / math.sqrt(tok_count * n_dp)
    x_blocks = activations.reshape(local_blocks, WIDTH, tok_count)
    g_blocks = cotangent.reshape(local_blocks, WIDTH, tok_count)
    g_cols = lax.all_to_all(g_blocks, "feat", split_axis=1, concat_axis=0, tiled=True)
    local_cols = l_mix.shape[0]
    rows_r = r_mix.shape[1]
    r_flat = r_mix.reshape(1, -1)
    packed = jnp.concatenate([r_flat, l_mix.reshape(1, -1)], axis=1)
    packed = lax.all_gather(packed, "dp", axis=0, tiled=True)
    r_size = r_flat.shape[1]
    r_whole = packed[:, :r_size].reshape(n_dp, local_blocks, rows_r, WIDTH)
    r_whole = jnp.transpose(r_whole, (1, 0, 2, 3)).reshape(local_blocks, n_dp * rows_r, WIDTH)
    l_whole = packed[:, r_size:].reshape(n_dp, local_cols, -1, BLOCKS)
    l_blocks = jnp.transpose(l_whole, (0, 2, 1, 3)).reshape(-1, local_cols, BLOCKS)
    mixed_rows = jnp.einsum(
        "bit,bio->bot", x_blocks, r_whole, preferred_element_type=jnp.float32
    ).astype(jnp.bfloat16)
    columns = lax.all_to_all(mixed_rows, "feat", split_axis=1, concat_axis=0, tiled=True)
    pre_act = jnp.einsum("bst,bsc->cst", columns, l_blocks, preferred_element_type=jnp.float32)
    slope_cols = slope_of(pre_act, g_cols)
    back_cols = jnp.einsum(
        "cst,bsc->sbt", slope_cols, l_blocks, preferred_element_type=jnp.float32
    ).astype(jnp.bfloat16)
    l_term = jnp.einsum("bst,cst->bsc", columns, slope_cols, preferred_element_type=jnp.float32)
    l_term = (l_term * grad_scale).reshape(n_dp, -1, local_cols, BLOCKS)
    grad_l = ring_reduce_scatter(l_term, ring)
    grad_l = jnp.transpose(grad_l, (1, 0, 2)).reshape(local_cols, -1)
    back_rows = lax.all_to_all(back_cols, "feat", split_axis=1, concat_axis=0, tiled=True)
    through_r = jnp.einsum("obt,bio->bit", back_rows, r_whole, preferred_element_type=jnp.float32)
    grad_x = (
        (g_blocks.astype(jnp.float32) + through_r)
        .astype(jnp.bfloat16)
        .reshape(local_blocks * WIDTH, tok_count)
    )
    r_term = (
        jnp.einsum("bit,obt->ibo", x_blocks, back_rows, preferred_element_type=jnp.float32)
        * grad_scale
    ).reshape(n_dp, rows_r, local_blocks, WIDTH)
    grad_r = ring_reduce_scatter(r_term, ring)
    grad_r = jnp.transpose(grad_r, (1, 0, 2))
    return (grad_x, grad_r, grad_l)


def solution(mesh):
    ring = ring_of(mesh)
    placed = (P("feat", "dp"), P("feat", "dp"), P("feat", "dp", None), P("feat", "dp"))
    return jax.shard_map(
        lambda *args: body(ring, *args),
        mesh=mesh,
        in_specs=placed,
        out_specs=(P("feat", "dp"), P("feat", "dp", None), P("feat", "dp")),
        check_vma=False,
    )
```

profile of v0, /device:TPU:0, one launch (start us, length us, event | category | flops | bytes accessed | tf_op | source)
XLA Modules:
  0.0 299.4 jit_solution(11265219353165768789)
XLA Ops:
  7.2 1.1 copy.50
  8.3 1.0 reshape.111
  9.4 3.6 %maximum_bitcast_fusion = bf16[1,1,163840]{2,1,0:T(2,128)(2,1)} fusion(bf16[1,32768]{1,0:T(2,128)(2,1)S(1)} %bitcast.189, bf16[1,131072]{1,0:T(2,128)(2,1)S(1)} %reshape.111), kind=kLoop, calls=%fused_computation.22 | loop fusion | flops 655360 | bytes 655360
  13.0 4.1 %copy.37 = bf16[16,256,256]{2,0,1:T(8,128)(2,1)} copy(bf16[16,256,256]{2,1,0:T(8,128)(2,1)} %bitcast.183) | data formatting | bytes 4194304 | tf_op jit(solution)/shard_map/reshape | solution.py:83
  17.1 4.5 %all-to-all-start = ((bf16[16,256,256]{2,0,1:T(8,128)(2,1)}), bf16[16,256,256]{2,0,1:T(8,128)(2,1)}, u32[]{:S(2)}, u32[]{:S(2)}) async-start(bf16[16,256,256]{2,0,1:T(8,128)(2,1)} %copy.37), calls=%async_computation | async-start | bytes 4194304 | tf_op jit(solution)/shard_map/all_to_all | solution.py:84
  21.6 80.6 %all-gather.3.cloned.1.call-done = bf16[8,1,163840]{2,1,0:T(2,128)(2,1)} async-done(((bf16[1,1,163840]{2,1,0:T(2,128)(2,1)}), bf16[8,1,163840]{2,1,0:T(2,128)(2,1)}) %all-gather.3.cloned.1.call-update) | async-done | bytes 2621456 | tf_op jit(solution)/shard_map/all_gather | solution.py:89
  102.1 5.8 %copy.58 = bf16[8,1,163840]{2,0,1:T(8,128)(2,1)S(1)} copy(bf16[8,1,163840]{2,1,0:T(2,128)(2,1)} %all-gather.3.cloned.1.call-done) | data formatting | bytes 5242880
  108.1 1.4 copy-done.3
  111.5 2.5 copy.40
  114.0 4.8 %all-to-all-start.1 = ((bf16[16,256,256]{2,0,1:T(8,128)(2,1)}), bf16[16,256,256]{2,0,1:T(8,128)(2,1)}, u32[]{:S(2)}, u32[]{:S(2)}) async-start(bf16[16,256,256]{2,0,1:T(8,128)(2,1)} %copy.40), calls=%async_computation.1 | async-start | bytes 4194304 | tf_op jit(solution)/shard_map/all_to_all | solution.py:98
  160.8 4.2 %copy.38 = f32[16,4,64,256]{3,0,1,2:T(8,128)} copy(bf16[16,4,64,256]{3,0,2,1:T(8,128)(2,1)} %bitcast.92) | data formatting | bytes 6291456 | tf_op jit(solution)/shard_map/convert_element_type | solution.py:18
  164.9 1.1 slice.25
  166.0 2.1 reshape.115
  168.1 1.5 copy.36
  169.6 2.0 copy.41
  172.4 5.1 %fusion.6 = bf16[64,64,256]{2,0,1:T(8,128)(2,1)S(1)} fusion(f32[16,4,64,256]{3,0,1,2:T(8,128)S(1)} %copy-done.6, bf16[64,64,256]{2,0,1:T(8,128)(2,1)S(1)} %bitcast.179, bf16[64,64,64]{2,1,0:T(8,128)(2,1)S(1)} %bitcast.185), kind=kOutput, calls=%fused_computation.8 | convolution fusion | flops 155189248 | bytes 8912896 | tf_op jit(solution)/shard_map/bst,bsc->cst/dot_general | solution.py:99
  177.5 2.0 multiply_bitcast_fusion
  179.5 1.3 convolution_convert_fusion
  180.8 2.5 copy.44
  183.4 3.8 %copy.46 = f32[64,64,64]{2,1,0:T(8,128)} copy(f32[64,64,64]{0,2,1:T(8,128)} %multiply_bitcast_fusion) | data formatting | bytes 2097152 | tf_op jit(solution)/shard_map/mul | solution.py:105
  187.2 2.7 fusion.13
  189.9 4.5 %all-to-all-start.2 = ((bf16[64,64,256]{2,0,1:T(8,128)(2,1)}), bf16[64,64,256]{2,0,1:T(8,128)(2,1)}, u32[]{:S(2)}, u32[]{:S(2)}) async-start(bf16[64,64,256]{2,0,1:T(8,128)(2,1)} %copy.44), calls=%async_computation.2 | async-start | bytes 4194304 | tf_op jit(solution)/shard_map/all_to_all | solution.py:108
  194.3 0.9 dynamic-slice_bitcast_fusion.2
  195.7 1.7 collective-permute-start.14
  197.4 3.8 %collective-permute-done.21 = f32[4,64,64]{2,1,0:T(8,128)S(1)} collective-permute-done((f32[4,64,64]{2,1,0:T(8,128)S(1)}, f32[4,64,64]{2,1,0:T(8,128)S(1)}, u32[]{:S(2)}, u32[]{:S(2)}) %collective-permute-start.21) | collective-permute-done | bytes 65568 | tf_op jit(solution)/shard_map/ppermute | solution.py:72
  201.2 0.9 bitcast_add_fusion.20
  202.6 1.7 collective-permute-start.15
  204.3 3.1 %collective-permute-done.22 = f32[4,64,64]{2,1,0:T(8,128)S(1)} collective-permute-done((f32[4,64,64]{2,1,0:T(8,128)S(1)}, f32[4,64,64]{2,1,0:T(8,128)S(1)}, u32[]{:S(2)}, u32[]{:S(2)}) %collective-permute-start.22) | collective-permute-done | bytes 65568 | tf_op jit(solution)/shard_map/ppermute | solution.py:72
  207.3 0.9 bitcast_add_fusion.19
  208.7 1.7 collective-permute-start.16
  210.4 2.9 collective-permute-done.23
  213.3 0.9 bitcast_add_fusion.18
  214.7 1.7 collective-permute-start.17
  216.4 2.9 collective-permute-done.24
  219.2 0.9 bitcast_add_fusion.17
  220.6 1.7 collective-permute-start.18
  222.3 2.9 collective-permute-done.25
  225.2 0.9 bitcast_add_fusion.16
  226.6 1.8 copy.45
  230.5 1.7 collective-permute-start.7
  232.6 0.9 bitcast_add_fusion.23
  233.5 1.7 collective-permute-start.19
  235.2 2.4 collective-permute-done.7
  237.7 2.6 collective-permute-start.8
  240.5 0.9 bitcast_add_fusion.15
  241.4 2.1 collective-permute-start.27
  243.5 3.2 %collective-permute-done.8 = f32[16,16,256]{2,0,1:T(8,128)S(1)} collective-permute-done((f32[16,16,256]{2,0,1:T(8,128)S(1)}, f32[16,16,256]{2,0,1:T(8,128)S(1)}, u32[]{:S(2)}, u32[]{:S(2)}) %collective-permute-start.8) | collective-permute-done | bytes 262176 | tf_op jit(solution)/shard_map/ppermute | solution.py:72
  246.8 2.5 collective-permute-start.9
  249.4 1.6 collective-permute-start.20
  251.0 4.7 %collective-permute-done.9 = f32[16,16,256]{2,0,1:T(8,128)S(1)} collective-permute-done((f32[16,16,256]{2,0,1:T(8,128)S(1)}, f32[16,16,256]{2,0,1:T(8,128)S(1)}, u32[]{:S(2)}, u32[]{:S(2)}) %collective-permute-start.9) | collective-permute-done | bytes 262176 | tf_op jit(solution)/shard_map/ppermute | solution.py:72
  255.8 2.5 collective-permute-start.10
  258.5 0.9 bitcast_add_fusion.14
  259.4 5.3 %collective-permute-done.10 = f32[16,16,256]{2,0,1:T(8,128)S(1)} collective-permute-done((f32[16,16,256]{2,0,1:T(8,128)S(1)}, f32[16,16,256]{2,0,1:T(8,128)S(1)}, u32[]{:S(2)}, u32[]{:S(2)}) %collective-permute-start.10) | collective-permute-done | bytes 262176 | tf_op jit(solution)/shard_map/ppermute | solution.py:72
  264.7 1.7 collective-permute-start.11
  266.9 5.8 %collective-permute-done.11 = f32[16,16,256]{2,0,1:T(8,128)S(1)} collective-permute-done((f32[16,16,256]{2,0,1:T(8,128)S(1)}, f32[16,16,256]{2,0,1:T(8,128)S(1)}, u32[]{:S(2)}, u32[]{:S(2)}) %collective-permute-start.11) | collective-permute-done | bytes 262176 | tf_op jit(solution)/shard_map/ppermute | solution.py:72
  272.7 1.0 collective-permute-start.12
  273.8 1.1 collective-permute-start.5
  275.9 4.9 %collective-permute-done.12 = f32[16,16,256]{2,0,1:T(8,128)S(1)} collective-permute-done((f32[16,16,256]{2,0,1:T(8,128)S(1)}, f32[16,16,256]{2,0,1:T(8,128)S(1)}, u32[]{:S(2)}, u32[]{:S(2)}) %collective-permute-start.12) | collective-permute-done | bytes 262176 | tf_op jit(solution)/shard_map/ppermute | solution.py:72
  280.7 1.0 bitcast_add_fusion.1
  282.1 1.0 bitcast_add_fusion.8
  283.1 1.8 collective-permute-start.6
  284.9 4.9 %add_convert_fusion = bf16[16,256,256]{2,1,0:T(8,128)(2,1)} fusion(bf16[16,256,256]{2,1,0:T(8,128)(2,1)} %bitcast.184, bf16[16,256,256]{2,1,0:T(8,128)(2,1)} %bitcast.173, bf16[256,16,256]{2,0,1:T(8,128)(2,1)} %bitcast.175), kind=kOutput, calls=%fused_computation.14 | convolution fusion | flops 540016640 | bytes 8388608 | tf_op jit(solution)/shard_map/obt,bio->bit/dot_general | solution.py:109
  289.8 1.0 bitcast_add_fusion
  290.8 1.0 bitcast_add_fusion.7
  (81 shorter events, 12.8 us)
Async XLA Ops:
  7.2 102.9 %copy-start = (bf16[4096,256]{1,0:T(8,128)(2,1)S(1)}, bf16[4096,256]{1,0:T(8,128)(2,1)}, u32[]{:S(2)}) copy-start(bf16[4096,256]{1,0:T(8,128)(2,1)} %param.8) | copy-start | bytes 6291460
  7.2 94.9 %all-gather.3.cloned.1.call-start = ((), (), s32[]{:S(2)}) async-start(), calls=%async_computation.3 | async-start | bytes 5898240 | tf_op jit(solution)/shard_map/all_gather | solution.py:89
  17.1 96.9 %all-to-all-start = ((bf16[16,256,256]{2,0,1:T(8,128)(2,1)}), bf16[16,256,256]{2,0,1:T(8,128)(2,1)}, u32[]{:S(2)}, u32[]{:S(2)}) async-start(bf16[16,256,256]{2,0,1:T(8,128)(2,1)} %copy.37), calls=%async_computation | async-start | bytes 4194304 | tf_op jit(solution)/shard_map/all_to_all | solution.py:84
  108.0 1.5 copy-start.3
  110.1 1.4 copy-start.1
  114.0 4.8 %copy-start.8 = (s32[8]{0:T(128)S(1)}, s32[8]{0:T(128)}, u32[]{:S(2)}) copy-start(s32[8]{0:T(128)} %constant.327.clone) | copy-start | bytes 100
  114.0 16.1 %copy-start.7 = (s32[8]{0:T(128)S(1)}, s32[8]{0:T(128)}, u32[]{:S(2)}) copy-start(s32[8]{0:T(128)} %constant.326.clone) | copy-start | bytes 100
  114.0 55.6 %all-to-all-start.1 = ((bf16[16,256,256]{2,0,1:T(8,128)(2,1)}), bf16[16,256,256]{2,0,1:T(8,128)(2,1)}, u32[]{:S(2)}, u32[]{:S(2)}) async-start(bf16[16,256,256]{2,0,1:T(8,128)(2,1)} %copy.40), calls=%async_computation.1 | async-start | bytes 4194304 | tf_op jit(solution)/shard_map/all_to_all | solution.py:98
  169.6 2.8 copy-start.6
  189.9 36.7 %all-to-all-start.2 = ((bf16[64,64,256]{2,0,1:T(8,128)(2,1)}), bf16[64,64,256]{2,0,1:T(8,128)(2,1)}, u32[]{:S(2)}, u32[]{:S(2)}) async-start(bf16[64,64,256]{2,0,1:T(8,128)(2,1)} %copy.44), calls=%async_computation.2 | async-start | bytes 4194304 | tf_op jit(solution)/shard_map/all_to_all | solution.py:108
  195.3 5.9 %collective-permute-start.21 = (f32[4,64,64]{2,1,0:T(8,128)S(1)}, f32[4,64,64]{2,1,0:T(8,128)S(1)}, u32[]{:S(2)}, u32[]{:S(2)}) collective-permute-start(f32[4,64,64]{2,1,0:T(8,128)S(1)} %dynamic-slice_bitcast_fusion.2), channel_id=1, source_target_pairs={{0,8},{4,0},{12,4},{20,12},{28,20},{24,28},{16,24},{8,16},{1,9},{5... | collective-permute-start | bytes 196616 | tf_op jit(solution)/shard_map/ppermute | solution.py:72
  195.7 6.8 %collective-permute-start.14 = (f32[4,64,64]{2,1,0:T(8,128)S(1)}, f32[4,64,64]{2,1,0:T(8,128)S(1)}, u32[]{:S(2)}, u32[]{:S(2)}) collective-permute-start(f32[4,64,64]{2,1,0:T(8,128)S(1)} %dynamic-slice_bitcast_fusion.3), channel_id=1, source_target_pairs={{0,4},{4,12},{12,20},{20,28},{28,24},{24,16},{16,8},{8,0},{1,5},{5... | collective-permute-start | bytes 196616 | tf_op jit(solution)/shard_map/ppermute | solution.py:72
  202.1 5.2 %collective-permute-start.22 = (f32[4,64,64]{2,1,0:T(8,128)S(1)}, f32[4,64,64]{2,1,0:T(8,128)S(1)}, u32[]{:S(2)}, u32[]{:S(2)}) collective-permute-start(f32[4,64,64]{2,1,0:T(8,128)S(1)} %bitcast_add_fusion.20), channel_id=1, source_target_pairs={{0,8},{4,0},{12,4},{20,12},{28,20},{24,28},{16,24},{8,16},{1,9},{5... | collective-permute-start | bytes 196616 | tf_op jit(solution)/shard_map/ppermute | solution.py:72
  202.6 6.1 %collective-permute-start.15 = (f32[4,64,64]{2,1,0:T(8,128)S(1)}, f32[4,64,64]{2,1,0:T(8,128)S(1)}, u32[]{:S(2)}, u32[]{:S(2)}) collective-permute-start(f32[4,64,64]{2,1,0:T(8,128)S(1)} %bitcast_add_fusion.27), channel_id=1, source_target_pairs={{0,4},{4,12},{12,20},{20,28},{28,24},{24,16},{16,8},{8,0},{1,5},{5... | collective-permute-start | bytes 196616 | tf_op jit(solution)/shard_map/ppermute | solution.py:72
  208.3 5.0 %collective-permute-start.23 = (f32[4,64,64]{2,1,0:T(8,128)S(1)}, f32[4,64,64]{2,1,0:T(8,128)S(1)}, u32[]{:S(2)}, u32[]{:S(2)}) collective-permute-start(f32[4,64,64]{2,1,0:T(8,128)S(1)} %bitcast_add_fusion.19), channel_id=1, source_target_pairs={{0,8},{4,0},{12,4},{20,12},{28,20},{24,28},{16,24},{8,16},{1,9},{5... | collective-permute-start | bytes 196616 | tf_op jit(solution)/shard_map/ppermute | solution.py:72
  208.7 5.9 %collective-permute-start.16 = (f32[4,64,64]{2,1,0:T(8,128)S(1)}, f32[4,64,64]{2,1,0:T(8,128)S(1)}, u32[]{:S(2)}, u32[]{:S(2)}) collective-permute-start(f32[4,64,64]{2,1,0:T(8,128)S(1)} %bitcast_add_fusion.26), channel_id=1, source_target_pairs={{0,4},{4,12},{12,20},{20,28},{28,24},{24,16},{16,8},{8,0},{1,5},{5... | collective-permute-start | bytes 196616 | tf_op jit(solution)/shard_map/ppermute | solution.py:72
  214.2 5.0 %collective-permute-start.24 = (f32[4,64,64]{2,1,0:T(8,128)S(1)}, f32[4,64,64]{2,1,0:T(8,128)S(1)}, u32[]{:S(2)}, u32[]{:S(2)}) collective-permute-start(f32[4,64,64]{2,1,0:T(8,128)S(1)} %bitcast_add_fusion.18), channel_id=1, source_target_pairs={{0,8},{4,0},{12,4},{20,12},{28,20},{24,28},{16,24},{8,16},{1,9},{5... | collective-permute-start | bytes 196616 | tf_op jit(solution)/shard_map/ppermute | solution.py:72
  214.7 5.9 %collective-permute-start.17 = (f32[4,64,64]{2,1,0:T(8,128)S(1)}, f32[4,64,64]{2,1,0:T(8,128)S(1)}, u32[]{:S(2)}, u32[]{:S(2)}) collective-permute-start(f32[4,64,64]{2,1,0:T(8,128)S(1)} %bitcast_add_fusion.25), channel_id=1, source_target_pairs={{0,4},{4,12},{12,20},{20,28},{28,24},{24,16},{16,8},{8,0},{1,5},{5... | collective-permute-start | bytes 196616 | tf_op jit(solution)/shard_map/ppermute | solution.py:72
  220.1 5.1 %collective-permute-start.25 = (f32[4,64,64]{2,1,0:T(8,128)S(1)}, f32[4,64,64]{2,1,0:T(8,128)S(1)}, u32[]{:S(2)}, u32[]{:S(2)}) collective-permute-start(f32[4,64,64]{2,1,0:T(8,128)S(1)} %bitcast_add_fusion.17), channel_id=1, source_target_pairs={{0,8},{4,0},{12,4},{20,12},{28,20},{24,28},{16,24},{8,16},{1,9},{5... | collective-permute-start | bytes 196616 | tf_op jit(solution)/shard_map/ppermute | solution.py:72
  220.6 12.0 %collective-permute-start.18 = (f32[4,64,64]{2,1,0:T(8,128)S(1)}, f32[4,64,64]{2,1,0:T(8,128)}, u32[]{:S(2)}, u32[]{:S(2)}) collective-permute-start(f32[4,64,64]{2,1,0:T(8,128)S(1)} %bitcast_add_fusion.24), channel_id=1, source_target_pairs={{0,4},{4,12},{12,20},{20,28},{28,24},{24,16},{16,8},{8,0},{1,5},{5... | collective-permute-start | bytes 196616 | tf_op jit(solution)/shard_map/ppermute | solution.py:72
  226.1 14.3 %collective-permute-start.26 = (f32[4,64,64]{2,1,0:T(8,128)S(1)}, f32[4,64,64]{2,1,0:T(8,128)S(1)}, u32[]{:S(2)}, u32[]{:S(2)}) collective-permute-start(f32[4,64,64]{2,1,0:T(8,128)S(1)} %bitcast_add_fusion.16), channel_id=1, source_target_pairs={{0,8},{4,0},{12,4},{20,12},{28,20},{24,28},{16,24},{8,16},{1,9},{5... | collective-permute-start | bytes 196616 | tf_op jit(solution)/shard_map/ppermute | solution.py:72
  228.4 1.3 copy-start.2
  230.4 42.3 %copy-start.5 = (f32[8,16,16,256]{3,1,0,2:T(8,128)}, f32[8,16,16,256]{3,1,0,2:T(8,128)S(1)}, u32[]{:S(2)}) copy-start(f32[8,16,16,256]{3,1,0,2:T(8,128)S(1)} %get-tuple-element.4) | copy-start | bytes 6291460
  230.4 43.4 %copy-start.4 = (f32[8,16,16,256]{3,1,0,2:T(8,128)}, f32[8,16,16,256]{3,1,0,2:T(8,128)S(1)}, u32[]{:S(2)}) copy-start(f32[8,16,16,256]{3,1,0,2:T(8,128)S(1)} %get-tuple-element.3) | copy-start | bytes 6291460
  230.5 7.2 %collective-permute-start.7 = (f32[16,16,256]{2,0,1:T(8,128)S(1)}, f32[16,16,256]{2,0,1:T(8,128)S(1)}, u32[]{:S(2)}, u32[]{:S(2)}) collective-permute-start(f32[16,16,256]{2,0,1:T(8,128)S(1)} %dynamic-slice_bitcast_fusion), channel_id=1, source_target_pairs={{0,8},{4,0},{12,4},{20,12},{28,20},{24,28},{16,24},{8,16},{1,9},{5... | collective-permute-start | bytes 786440 | tf_op jit(solution)/shard_map/ppermute | solution.py:72
  232.2 8.2 %collective-permute-start = (f32[16,16,256]{2,0,1:T(8,128)S(1)}, f32[16,16,256]{2,0,1:T(8,128)S(1)}, u32[]{:S(2)}, u32[]{:S(2)}) collective-permute-start(f32[16,16,256]{2,0,1:T(8,128)S(1)} %dynamic-slice_bitcast_fusion.1), channel_id=1, source_target_pairs={{0,4},{4,12},{12,20},{20,28},{28,24},{24,16},{16,8},{8,0},{1,5},{5... | collective-permute-start | bytes 786440 | tf_op jit(solution)/shard_map/ppermute | solution.py:72
  233.5 15.9 %collective-permute-start.19 = (f32[4,64,64]{2,1,0:T(8,128)S(1)}, f32[4,64,64]{2,1,0:T(8,128)S(1)}, u32[]{:S(2)}, u32[]{:S(2)}) collective-permute-start(f32[4,64,64]{2,1,0:T(8,128)S(1)} %bitcast_add_fusion.23), channel_id=1, source_target_pairs={{0,4},{4,12},{12,20},{20,28},{28,24},{24,16},{16,8},{8,0},{1,5},{5... | collective-permute-start | bytes 196616 | tf_op jit(solution)/shard_map/ppermute | solution.py:72
  237.7 9.0 %collective-permute-start.8 = (f32[16,16,256]{2,0,1:T(8,128)S(1)}, f32[16,16,256]{2,0,1:T(8,128)S(1)}, u32[]{:S(2)}, u32[]{:S(2)}) collective-permute-start(f32[16,16,256]{2,0,1:T(8,128)S(1)} %bitcast_add_fusion.6), channel_id=1, source_target_pairs={{0,8},{4,0},{12,4},{20,12},{28,20},{24,28},{16,24},{8,16},{1,9},{5... | collective-permute-start | bytes 786440 | tf_op jit(solution)/shard_map/ppermute | solution.py:72
  240.4 8.9 %collective-permute-start.1 = (f32[16,16,256]{2,0,1:T(8,128)S(1)}, f32[16,16,256]{2,0,1:T(8,128)S(1)}, u32[]{:S(2)}, u32[]{:S(2)}) collective-permute-start(f32[16,16,256]{2,0,1:T(8,128)S(1)} %bitcast_add_fusion.13), channel_id=1, source_target_pairs={{0,4},{4,12},{12,20},{20,28},{28,24},{24,16},{16,8},{8,0},{1,5},{5... | collective-permute-start | bytes 786440 | tf_op jit(solution)/shard_map/ppermute | solution.py:72
  241.4 17.0 %collective-permute-start.27 = (f32[4,64,64]{2,1,0:T(8,128)S(1)}, f32[4,64,64]{2,1,0:T(8,128)S(1)}, u32[]{:S(2)}, u32[]{:S(2)}) collective-permute-start(f32[4,64,64]{2,1,0:T(8,128)S(1)} %bitcast_add_fusion.15), channel_id=1, source_target_pairs={{0,8},{4,0},{12,4},{20,12},{28,20},{24,28},{16,24},{8,16},{1,9},{5... | collective-permute-start | bytes 196616 | tf_op jit(solution)/shard_map/ppermute | solution.py:72
  246.8 9.0 %collective-permute-start.9 = (f32[16,16,256]{2,0,1:T(8,128)S(1)}, f32[16,16,256]{2,0,1:T(8,128)S(1)}, u32[]{:S(2)}, u32[]{:S(2)}) collective-permute-start(f32[16,16,256]{2,0,1:T(8,128)S(1)} %bitcast_add_fusion.5), channel_id=1, source_target_pairs={{0,8},{4,0},{12,4},{20,12},{28,20},{24,28},{16,24},{8,16},{1,9},{5... | collective-permute-start | bytes 786440 | tf_op jit(solution)/shard_map/ppermute | solution.py:72
  249.3 9.0 %collective-permute-start.2 = (f32[16,16,256]{2,0,1:T(8,128)S(1)}, f32[16,16,256]{2,0,1:T(8,128)S(1)}, u32[]{:S(2)}, u32[]{:S(2)}) collective-permute-start(f32[16,16,256]{2,0,1:T(8,128)S(1)} %bitcast_add_fusion.12), channel_id=1, source_target_pairs={{0,4},{4,12},{12,20},{20,28},{28,24},{24,16},{16,8},{8,0},{1,5},{5... | collective-permute-start | bytes 786440 | tf_op jit(solution)/shard_map/ppermute | solution.py:72
  249.4 17.5 %collective-permute-start.20 = (f32[4,64,64]{2,1,0:T(8,128)S(1)}, f32[4,64,64]{2,1,0:T(8,128)S(1)}, u32[]{:S(2)}, u32[]{:S(2)}) collective-permute-start(f32[4,64,64]{2,1,0:T(8,128)S(1)} %bitcast_add_fusion.22), channel_id=1, source_target_pairs={{0,4},{4,12},{12,20},{20,28},{28,24},{24,16},{16,8},{8,0},{1,5},{5... | collective-permute-start | bytes 196616 | tf_op jit(solution)/shard_map/ppermute | solution.py:72
  255.8 8.9 %collective-permute-start.10 = (f32[16,16,256]{2,0,1:T(8,128)S(1)}, f32[16,16,256]{2,0,1:T(8,128)S(1)}, u32[]{:S(2)}, u32[]{:S(2)}) collective-permute-start(f32[16,16,256]{2,0,1:T(8,128)S(1)} %bitcast_add_fusion.4), channel_id=1, source_target_pairs={{0,8},{4,0},{12,4},{20,12},{28,20},{24,28},{16,24},{8,16},{1,9},{5... | collective-permute-start | bytes 786440 | tf_op jit(solution)/shard_map/ppermute | solution.py:72
  258.3 8.1 %collective-permute-start.3 = (f32[16,16,256]{2,0,1:T(8,128)S(1)}, f32[16,16,256]{2,0,1:T(8,128)S(1)}, u32[]{:S(2)}, u32[]{:S(2)}) collective-permute-start(f32[16,16,256]{2,0,1:T(8,128)S(1)} %bitcast_add_fusion.11), channel_id=1, source_target_pairs={{0,4},{4,12},{12,20},{20,28},{28,24},{24,16},{16,8},{8,0},{1,5},{5... | collective-permute-start | bytes 786440 | tf_op jit(solution)/shard_map/ppermute | solution.py:72
  264.7 8.0 %collective-permute-start.11 = (f32[16,16,256]{2,0,1:T(8,128)S(1)}, f32[16,16,256]{2,0,1:T(8,128)S(1)}, u32[]{:S(2)}, u32[]{:S(2)}) collective-permute-start(f32[16,16,256]{2,0,1:T(8,128)S(1)} %bitcast_add_fusion.3), channel_id=1, source_target_pairs={{0,8},{4,0},{12,4},{20,12},{28,20},{24,28},{16,24},{8,16},{1,9},{5... | collective-permute-start | bytes 786440 | tf_op jit(solution)/shard_map/ppermute | solution.py:72
  266.5 7.3 %collective-permute-start.4 = (f32[16,16,256]{2,0,1:T(8,128)S(1)}, f32[16,16,256]{2,0,1:T(8,128)S(1)}, u32[]{:S(2)}, u32[]{:S(2)}) collective-permute-start(f32[16,16,256]{2,0,1:T(8,128)S(1)} %bitcast_add_fusion.10), channel_id=1, source_target_pairs={{0,4},{4,12},{12,20},{20,28},{28,24},{24,16},{16,8},{8,0},{1,5},{5... | collective-permute-start | bytes 786440 | tf_op jit(solution)/shard_map/ppermute | solution.py:72
  272.7 8.0 %collective-permute-start.12 = (f32[16,16,256]{2,0,1:T(8,128)S(1)}, f32[16,16,256]{2,0,1:T(8,128)S(1)}, u32[]{:S(2)}, u32[]{:S(2)}) collective-permute-start(f32[16,16,256]{2,0,1:T(8,128)S(1)} %bitcast_add_fusion.2), channel_id=1, source_target_pairs={{0,8},{4,0},{12,4},{20,12},{28,20},{24,28},{16,24},{8,16},{1,9},{5... | collective-permute-start | bytes 786440 | tf_op jit(solution)/shard_map/ppermute | solution.py:72
  273.8 8.3 %collective-permute-start.5 = (f32[16,16,256]{2,0,1:T(8,128)S(1)}, f32[16,16,256]{2,0,1:T(8,128)S(1)}, u32[]{:S(2)}, u32[]{:S(2)}) collective-permute-start(f32[16,16,256]{2,0,1:T(8,128)S(1)} %bitcast_add_fusion.9), channel_id=1, source_target_pairs={{0,4},{4,12},{12,20},{20,28},{28,24},{24,16},{16,8},{8,0},{1,5},{5... | collective-permute-start | bytes 786440 | tf_op jit(solution)/shard_map/ppermute | solution.py:72
  281.7 8.0 %collective-permute-start.13 = (f32[16,16,256]{2,0,1:T(8,128)S(1)}, f32[16,16,256]{2,0,1:T(8,128)S(1)}, u32[]{:S(2)}, u32[]{:S(2)}) collective-permute-start(f32[16,16,256]{2,0,1:T(8,128)S(1)} %bitcast_add_fusion.1), channel_id=1, source_target_pairs={{0,8},{4,0},{12,4},{20,12},{28,20},{24,28},{16,24},{8,16},{1,9},{5... | collective-permute-start | bytes 786440 | tf_op jit(solution)/shard_map/ppermute | solution.py:72
  283.1 7.7 %collective-permute-start.6 = (f32[16,16,256]{2,0,1:T(8,128)S(1)}, f32[16,16,256]{2,0,1:T(8,128)S(1)}, u32[]{:S(2)}, u32[]{:S(2)}) collective-permute-start(f32[16,16,256]{2,0,1:T(8,128)S(1)} %bitcast_add_fusion.8), channel_id=1, source_target_pairs={{0,4},{4,12},{12,20},{20,28},{28,24},{24,16},{16,8},{8,0},{1,5},{5... | collective-permute-start | bytes 786440 | tf_op jit(solution)/shard_map/ppermute | solution.py:72
Sparse Core Ops, SparseCore 0:
  13.1 88.9 all-gather.2
where the time goes:
time: 301 us; the launch traced here: 299 us
  waiting for transfers between devices  122 us (41%)
  between operations  55.1 us (18%)
  starting transfers between devices  46.6 us (15%)
  local copies, waits for them, and re-layouts  44.2 us (15%)
  other arithmetic  16.3 us (5%)
  matrix products  14.8 us (5%)
    all_gather x1, waiting for transfers between devices, body(): packed = lax.all_gather(packed, 'dp', axis=0, tiled=True)  80.6 us
    ppermute x28, waiting for transfers between devices, ring_reduce_scatter(): acc = lax.ppermute(acc, 'dp', pairs)  41.8 us
    ppermute x28, starting transfers between devices, ring_reduce_scatter(): acc = lax.ppermute(acc, 'dp', pairs)  32.9 us
    add x28, other arithmetic, ring_reduce_scatter(): acc = mine if acc is None else acc + mine  11.8 us
    unnamed x20, local copies, waits for them, and re-layouts  10.3 us
  transfers between devices with their start and end apart: 32, of which 13 were waited for; matrix products, arithmetic and copies ran while one was open for 15% of the time, Pallas kernels for 0%

commit v1 on v0

--- a/solution.py
+++ b/solution.py
@@ -86,7 +86,13 @@
     rows_r = r_mix.shape[1]
     r_flat = r_mix.reshape(1, -1)
     packed = jnp.concatenate([r_flat, l_mix.reshape(1, -1)], axis=1)
-    packed = lax.all_gather(packed, "dp", axis=0, tiled=True)
+    count = lax.axis_size("dp")
+    current, pieces = (packed, [packed])
+    for _ in range(count - 1):
+        current = lax.ppermute(current, "dp", [(i_2, (i_2 + 1) % count) for i_2 in range(count)])
+        pieces.insert(0, current)
+    line = jnp.concatenate(pieces, axis=0)
+    packed = jnp.roll(line, (lax.axis_index("dp") + 1) * packed.shape[0], axis=0)
     r_size = r_flat.shape[1]
     r_whole = packed[:, :r_size].reshape(n_dp, local_blocks, rows_r, WIDTH)
     r_whole = jnp.transpose(r_whole, (1, 0, 2, 3)).reshape(local_blocks, n_dp * rows_r, WIDTH)

time: 301 us -> 342 us (1.14)
  local copies, waits for them, and re-layouts: 44.2 us -> 72.2 us
  waiting for transfers between devices: 122 us -> 150 us
  between operations: 55.1 us -> 41.4 us
  other arithmetic: 16.3 us -> 12.7 us
    ppermute x0 -> x7, waiting for transfers between devices: none -> 107 us  [body(): lax.ppermute(current, 'dp', [(i_2, (i_2 + 1) % count) for i_2 in range(co...]
    all_gather x1 -> x0, waiting for transfers between devices: 80.6 us -> none  [body(): packed = lax.all_gather(packed, 'dp', axis=0, tiled=True)]
    concatenate x0 -> x2, local copies, waits for them, and re-layouts: none -> 28.1 us  [the longest x1 28 us: body(): jnp.roll(line, (lax.axis_index('dp') + 1) * packed.shape[0], axis=0)]
    unnamed x1 -> x0, other arithmetic: 3.62 us -> none
    unnamed x20 -> x26, local copies, waits for them, and re-layouts: 10.3 us -> 7.01 us
  transfers between devices with their start and end apart: 32 -> 38, of which waited for: 13 -> 19; matrix products, arithmetic and copies ran while one was open for 15% -> 21% of each run, Pallas kernels for 0% -> 0%
where the time goes in v1:
time: 342 us; the launch traced here: 338 us
  waiting for transfers between devices  150 us (44%)
  local copies, waits for them, and re-layouts  72.2 us (21%)
  starting transfers between devices  47.1 us (14%)
  between operations  41.4 us (12%)
  matrix products  14.9 us (4%)
  other arithmetic  12.7 us (4%)
    ppermute x7, waiting for transfers between devices, body(): lax.ppermute(current, 'dp', [(i_2, (i_2 + 1) % count) for i_2 in range(co...  107 us
    ppermute x28, waiting for transfers between devices, ring_reduce_scatter(): acc = lax.ppermute(acc, 'dp', pairs)  42 us
    ppermute x28, starting transfers between devices, ring_reduce_scatter(): acc = lax.ppermute(acc, 'dp', pairs)  30.4 us
    concatenate x1, local copies, waits for them, and re-layouts, body(): jnp.roll(line, (lax.axis_index('dp') + 1) * packed.shape[0], axis=0)  28 us
    add x28, other arithmetic, ring_reduce_scatter(): acc = mine if acc is None else acc + mine  11.8 us
    unnamed x26, local copies, waits for them, and re-layouts  7.01 us
  transfers between devices with their start and end apart: 38, of which 19 were waited for; matrix products, arithmetic and copies ran while one was open for 21% of the time, Pallas kernels for 0%

profile of v1, /device:TPU:0, one launch (start us, length us, event | category | flops | bytes accessed | tf_op | source)
XLA Modules:
  0.0 337.8 jit_solution(312702770908409246)
XLA Ops:
  0.6 1.1 copy.49
  1.7 1.0 reshape.111
  3.5 3.0 collective-permute-start
  6.5 17.8 %collective-permute-done = bf16[1,163840]{1,0:T(2,128)(2,1)S(1)} collective-permute-done((bf16[1,163840]{1,0:T(2,128)(2,1)S(1)}, bf16[1,163840]{1,0:T(2,128)(2,1)S(1)}, u32[]{:S(2)}, u32[]{:S(2)}) %collective-permute-start) | collective-permute-done | bytes 327712 | tf_op jit(solution)/shard_map/ppermute | solution.py:92
  24.3 18.6 %collective-permute-done.1 = bf16[1,163840]{1,0:T(2,128)(2,1)S(1)} collective-permute-done((bf16[1,163840]{1,0:T(2,128)(2,1)S(1)}, bf16[1,163840]{1,0:T(2,128)(2,1)S(1)}, u32[]{:S(2)}, u32[]{:S(2)}) %collective-permute-start.1) | collective-permute-done | bytes 327712 | tf_op jit(solution)/shard_map/ppermute | solution.py:92
  43.7 17.7 %collective-permute-done.2 = bf16[1,163840]{1,0:T(2,128)(2,1)S(1)} collective-permute-done((bf16[1,163840]{1,0:T(2,128)(2,1)S(1)}, bf16[1,163840]{1,0:T(2,128)(2,1)S(1)}, u32[]{:S(2)}, u32[]{:S(2)}) %collective-permute-start.2) | collective-permute-done | bytes 327712 | tf_op jit(solution)/shard_map/ppermute | solution.py:92
  62.4 16.8 %collective-permute-done.3 = bf16[1,163840]{1,0:T(2,128)(2,1)S(1)} collective-permute-done((bf16[1,163840]{1,0:T(2,128)(2,1)S(1)}, bf16[1,163840]{1,0:T(2,128)(2,1)S(1)}, u32[]{:S(2)}, u32[]{:S(2)}) %collective-permute-start.3) | collective-permute-done | bytes 327712 | tf_op jit(solution)/shard_map/ppermute | solution.py:92
  80.0 15.8 %collective-permute-done.4 = bf16[1,163840]{1,0:T(2,128)(2,1)S(1)} collective-permute-done((bf16[1,163840]{1,0:T(2,128)(2,1)S(1)}, bf16[1,163840]{1,0:T(2,128)(2,1)S(1)}, u32[]{:S(2)}, u32[]{:S(2)}) %collective-permute-start.4) | collective-permute-done | bytes 327712 | tf_op jit(solution)/shard_map/ppermute | solution.py:92
  96.7 15.0 %collective-permute-done.5 = bf16[1,163840]{1,0:T(2,128)(2,1)} collective-permute-done((bf16[1,163840]{1,0:T(2,128)(2,1)S(1)}, bf16[1,163840]{1,0:T(2,128)(2,1)}, u32[]{:S(2)}, u32[]{:S(2)}) %collective-permute-start.5) | collective-permute-done | bytes 327712 | tf_op jit(solution)/shard_map/ppermute | solution.py:92
  111.8 4.1 %copy.37 = bf16[16,256,256]{2,0,1:T(8,128)(2,1)} copy(bf16[16,256,256]{2,1,0:T(8,128)(2,1)} %bitcast.176) | data formatting | bytes 4194304 | tf_op jit(solution)/shard_map/reshape | solution.py:83
  115.8 4.5 %all-to-all-start = ((bf16[16,256,256]{2,0,1:T(8,128)(2,1)}), bf16[16,256,256]{2,0,1:T(8,128)(2,1)}, u32[]{:S(2)}, u32[]{:S(2)}) async-start(bf16[16,256,256]{2,0,1:T(8,128)(2,1)} %copy.37), calls=%async_computation | async-start | bytes 4194304 | tf_op jit(solution)/shard_map/all_to_all | solution.py:84
  120.3 5.7 %collective-permute-done.6 = bf16[1,163840]{1,0:T(2,128)(2,1)} collective-permute-done((bf16[1,163840]{1,0:T(2,128)(2,1)}, bf16[1,163840]{1,0:T(2,128)(2,1)}, u32[]{:S(2)}, u32[]{:S(2)}) %collective-permute-start.6) | collective-permute-done | bytes 327712 | tf_op jit(solution)/shard_map/ppermute | solution.py:92
  126.1 28.0 %concatenate.16 = bf16[16,163840]{1,0:T(8,128)(2,1)} concatenate(bf16[1,163840]{1,0:T(2,128)(2,1)} %collective-permute-done.6, bf16[1,163840]{1,0:T(2,128)(2,1)} %collective-permute-done.5, bf16[1,163840]{1,0:T(2,128)(2,1)} %copy-done.9, bf16[1,163840]{1,0:T(2,128)(2,1)} %copy-done.8, bf16[1,163840]{1,0:T(2,128)(2,1)} %copy-done.7, bf16[1,163840]{1,0:T(2,128)(2,1)} %copy-done.6, ...), dimensions={0} | concatenate | bytes 10485760 | tf_op jit(solution)/shard_map/jit(_roll_dynamic)/concatenate | solution.py:95
  154.1 2.8 constant_dynamic-slice_fusion
  158.8 2.5 copy.40
  161.3 4.8 %all-to-all-start.1 = ((bf16[16,256,256]{2,0,1:T(8,128)(2,1)}), bf16[16,256,256]{2,0,1:T(8,128)(2,1)}, u32[]{:S(2)}, u32[]{:S(2)}) async-start(bf16[16,256,256]{2,0,1:T(8,128)(2,1)} %copy.40), calls=%async_computation.1 | async-start | bytes 4194304 | tf_op jit(solution)/shard_map/all_to_all | solution.py:104
  207.8 4.2 %copy.38 = f32[16,4,64,256]{3,0,1,2:T(8,128)} copy(bf16[16,4,64,256]{3,0,2,1:T(8,128)(2,1)} %bitcast.91) | data formatting | bytes 6291456 | tf_op jit(solution)/shard_map/convert_element_type | solution.py:18
  212.0 1.5 dynamic-slice.1
  213.5 2.1 reshape.115
  215.6 1.5 copy.36
  217.1 2.0 copy.41
  220.0 5.1 %fusion.6 = bf16[64,64,256]{2,0,1:T(8,128)(2,1)S(1)} fusion(f32[16,4,64,256]{3,0,1,2:T(8,128)S(1)} %copy-done.5, bf16[64,64,256]{2,0,1:T(8,128)(2,1)S(1)} %bitcast.172, bf16[64,64,64]{2,1,0:T(8,128)(2,1)S(1)} %bitcast.178), kind=kOutput, calls=%fused_computation.8 | convolution fusion | flops 155189248 | bytes 8912896 | tf_op jit(solution)/shard_map/bst,bsc->cst/dot_general | solution.py:105
  225.0 2.1 multiply_bitcast_fusion
  227.1 1.3 convolution_convert_fusion
  228.4 2.5 copy.44
  230.9 3.8 %copy.46 = f32[64,64,64]{2,1,0:T(8,128)} copy(f32[64,64,64]{0,2,1:T(8,128)} %multiply_bitcast_fusion) | data formatting | bytes 2097152 | tf_op jit(solution)/shard_map/mul | solution.py:111
  234.7 2.7 fusion.13
  237.4 4.4 %all-to-all-start.2 = ((bf16[64,64,256]{2,0,1:T(8,128)(2,1)}), bf16[64,64,256]{2,0,1:T(8,128)(2,1)}, u32[]{:S(2)}, u32[]{:S(2)}) async-start(bf16[64,64,256]{2,0,1:T(8,128)(2,1)} %copy.44), calls=%async_computation.2 | async-start | bytes 4194304 | tf_op jit(solution)/shard_map/all_to_all | solution.py:114
  242.9 2.1 collective-permute-start.21
  244.9 3.8 %collective-permute-done.28 = f32[4,64,64]{2,1,0:T(8,128)S(1)} collective-permute-done((f32[4,64,64]{2,1,0:T(8,128)S(1)}, f32[4,64,64]{2,1,0:T(8,128)S(1)}, u32[]{:S(2)}, u32[]{:S(2)}) %collective-permute-start.28) | collective-permute-done | bytes 65568 | tf_op jit(solution)/shard_map/ppermute | solution.py:72
  248.7 0.9 bitcast_add_fusion.20
  250.0 1.8 collective-permute-start.22
  251.8 3.1 collective-permute-done.29
  254.9 0.9 bitcast_add_fusion.19
  256.4 1.6 collective-permute-start.23
  257.9 2.9 collective-permute-done.30
  262.3 1.6 collective-permute-start.24
  263.9 2.9 collective-permute-done.31
  266.7 0.9 bitcast_add_fusion.17
  268.2 1.6 collective-permute-start.25
  269.8 2.9 collective-permute-done.32
  274.4 1.8 copy.45
  278.6 1.8 collective-permute-start.7
  281.3 1.6 collective-permute-start.26
  283.0 3.0 collective-permute-done.14
  286.7 2.1 collective-permute-start.8
  289.8 5.9 %collective-permute-done.15 = f32[16,16,256]{2,0,1:T(8,128)S(1)} collective-permute-done((f32[16,16,256]{2,0,1:T(8,128)S(1)}, f32[16,16,256]{2,0,1:T(8,128)S(1)}, u32[]{:S(2)}, u32[]{:S(2)}) %collective-permute-start.15) | collective-permute-done | bytes 262176 | tf_op jit(solution)/shard_map/ppermute | solution.py:72
  295.9 2.1 collective-permute-start.9
  298.0 2.2 collective-permute-start.27
  300.1 4.2 %collective-permute-done.16 = f32[16,16,256]{2,0,1:T(8,128)S(1)} collective-permute-done((f32[16,16,256]{2,0,1:T(8,128)S(1)}, f32[16,16,256]{2,0,1:T(8,128)S(1)}, u32[]{:S(2)}, u32[]{:S(2)}) %collective-permute-start.16) | collective-permute-done | bytes 262176 | tf_op jit(solution)/shard_map/ppermute | solution.py:72
  304.8 1.8 collective-permute-start.10
  306.6 0.9 bitcast_add_fusion.14
  307.5 4.7 %collective-permute-done.17 = f32[16,16,256]{2,0,1:T(8,128)S(1)} collective-permute-done((f32[16,16,256]{2,0,1:T(8,128)S(1)}, f32[16,16,256]{2,0,1:T(8,128)S(1)}, u32[]{:S(2)}, u32[]{:S(2)}) %collective-permute-start.17) | collective-permute-done | bytes 262176 | tf_op jit(solution)/shard_map/ppermute | solution.py:72
  312.9 1.5 collective-permute-start.11
  314.4 4.7 %collective-permute-done.18 = f32[16,16,256]{2,0,1:T(8,128)S(1)} collective-permute-done((f32[16,16,256]{2,0,1:T(8,128)S(1)}, f32[16,16,256]{2,0,1:T(8,128)S(1)}, u32[]{:S(2)}, u32[]{:S(2)}) %collective-permute-start.18) | collective-permute-done | bytes 262176 | tf_op jit(solution)/shard_map/ppermute | solution.py:72
  319.1 1.0 collective-permute-start.19
  320.2 1.1 collective-permute-start.12
  322.2 3.7 %collective-permute-done.19 = f32[16,16,256]{2,0,1:T(8,128)S(1)} collective-permute-done((f32[16,16,256]{2,0,1:T(8,128)S(1)}, f32[16,16,256]{2,0,1:T(8,128)S(1)}, u32[]{:S(2)}, u32[]{:S(2)}) %collective-permute-start.19) | collective-permute-done | bytes 262176 | tf_op jit(solution)/shard_map/ppermute | solution.py:72
  326.0 1.0 bitcast_add_fusion.1
  327.0 1.4 collective-permute-start.20
  328.4 1.0 bitcast_add_fusion.8
  330.1 4.9 %add_convert_fusion = bf16[16,256,256]{2,1,0:T(8,128)(2,1)} fusion(bf16[16,256,256]{2,1,0:T(8,128)(2,1)} %bitcast.177, bf16[16,256,256]{2,1,0:T(8,128)(2,1)} %bitcast.168, bf16[256,16,256]{2,0,1:T(8,128)(2,1)} %bitcast.170), kind=kOutput, calls=%fused_computation.14 | convolution fusion | flops 540016640 | bytes 8388608 | tf_op jit(solution)/shard_map/obt,bio->bit/dot_general | solution.py:115
  335.0 1.0 bitcast_add_fusion
  336.0 1.0 bitcast_add_fusion.7
  (99 shorter events, 22.7 us)
Async XLA Ops:
  0.6 156.8 %copy-start = (bf16[4096,256]{1,0:T(8,128)(2,1)S(1)}, bf16[4096,256]{1,0:T(8,128)(2,1)}, u32[]{:S(2)}) copy-start(bf16[4096,256]{1,0:T(8,128)(2,1)} %param.8) | copy-start | bytes 6291460
  3.5 20.8 %collective-permute-start = (bf16[1,163840]{1,0:T(2,128)(2,1)S(1)}, bf16[1,163840]{1,0:T(2,128)(2,1)S(1)}, u32[]{:S(2)}, u32[]{:S(2)}) collective-permute-start(bf16[1,163840]{1,0:T(2,128)(2,1)S(1)} %constant_dynamic-update-slice_fusion), channel_id=1, source_target_pairs={{0,4},{4,8},{8,12},{12,16},{16,20},{20,24},{24,28},{28,0},{1,5},{5... | collective-permute-start | bytes 983048 | tf_op jit(solution)/shard_map/ppermute | solution.py:92
  24.3 18.6 %collective-permute-start.1 = (bf16[1,163840]{1,0:T(2,128)(2,1)S(1)}, bf16[1,163840]{1,0:T(2,128)(2,1)S(1)}, u32[]{:S(2)}, u32[]{:S(2)}) collective-permute-start(bf16[1,163840]{1,0:T(2,128)(2,1)S(1)} %collective-permute-done), channel_id=1, source_target_pairs={{0,4},{4,8},{8,12},{12,16},{16,20},{20,24},{24,28},{28,0},{1,5},{5... | collective-permute-start | bytes 983048 | tf_op jit(solution)/shard_map/ppermute | solution.py:92
  42.9 0.8 copy-start.6
  43.7 17.7 %collective-permute-start.2 = (bf16[1,163840]{1,0:T(2,128)(2,1)S(1)}, bf16[1,163840]{1,0:T(2,128)(2,1)S(1)}, u32[]{:S(2)}, u32[]{:S(2)}) collective-permute-start(bf16[1,163840]{1,0:T(2,128)(2,1)S(1)} %collective-permute-done.1), channel_id=1, source_target_pairs={{0,4},{4,8},{8,12},{12,16},{16,20},{20,24},{24,28},{28,0},{1,5},{5... | collective-permute-start | bytes 983048 | tf_op jit(solution)/shard_map/ppermute | solution.py:92
  61.4 0.9 copy-start.7
  62.4 16.8 %collective-permute-start.3 = (bf16[1,163840]{1,0:T(2,128)(2,1)S(1)}, bf16[1,163840]{1,0:T(2,128)(2,1)S(1)}, u32[]{:S(2)}, u32[]{:S(2)}) collective-permute-start(bf16[1,163840]{1,0:T(2,128)(2,1)S(1)} %collective-permute-done.2), channel_id=1, source_target_pairs={{0,4},{4,8},{8,12},{12,16},{16,20},{20,24},{24,28},{28,0},{1,5},{5... | collective-permute-start | bytes 983048 | tf_op jit(solution)/shard_map/ppermute | solution.py:92
  79.1 0.9 copy-start.8
  80.0 15.9 %collective-permute-start.4 = (bf16[1,163840]{1,0:T(2,128)(2,1)S(1)}, bf16[1,163840]{1,0:T(2,128)(2,1)S(1)}, u32[]{:S(2)}, u32[]{:S(2)}) collective-permute-start(bf16[1,163840]{1,0:T(2,128)(2,1)S(1)} %collective-permute-done.3), channel_id=1, source_target_pairs={{0,4},{4,8},{8,12},{12,16},{16,20},{20,24},{24,28},{28,0},{1,5},{5... | collective-permute-start | bytes 983048 | tf_op jit(solution)/shard_map/ppermute | solution.py:92
  95.9 0.8 copy-start.9
  96.7 15.0 %collective-permute-start.5 = (bf16[1,163840]{1,0:T(2,128)(2,1)S(1)}, bf16[1,163840]{1,0:T(2,128)(2,1)}, u32[]{:S(2)}, u32[]{:S(2)}) collective-permute-start(bf16[1,163840]{1,0:T(2,128)(2,1)S(1)} %collective-permute-done.4), channel_id=1, source_target_pairs={{0,4},{4,8},{8,12},{12,16},{16,20},{20,24},{24,28},{28,0},{1,5},{5... | collective-permute-start | bytes 983048 | tf_op jit(solution)/shard_map/ppermute | solution.py:92
  111.8 14.3 %collective-permute-start.6 = (bf16[1,163840]{1,0:T(2,128)(2,1)}, bf16[1,163840]{1,0:T(2,128)(2,1)}, u32[]{:S(2)}, u32[]{:S(2)}) collective-permute-start(bf16[1,163840]{1,0:T(2,128)(2,1)} %collective-permute-done.5), channel_id=1, source_target_pairs={{0,4},{4,8},{8,12},{12,16},{16,20},{20,24},{24,28},{28,0},{1,5},{5... | collective-permute-start | bytes 983048 | tf_op jit(solution)/shard_map/ppermute | solution.py:92
  115.8 45.4 %all-to-all-start = ((bf16[16,256,256]{2,0,1:T(8,128)(2,1)}), bf16[16,256,256]{2,0,1:T(8,128)(2,1)}, u32[]{:S(2)}, u32[]{:S(2)}) async-start(bf16[16,256,256]{2,0,1:T(8,128)(2,1)} %copy.37), calls=%async_computation | async-start | bytes 4194304 | tf_op jit(solution)/shard_map/all_to_all | solution.py:84
  157.5 1.3 copy-start.1
  161.3 4.8 %copy-start.11 = (s32[8]{0:T(128)S(1)}, s32[8]{0:T(128)}, u32[]{:S(2)}) copy-start(s32[8]{0:T(128)} %constant.344.clone) | copy-start | bytes 100
  161.3 16.1 %copy-start.10 = (s32[8]{0:T(128)S(1)}, s32[8]{0:T(128)}, u32[]{:S(2)}) copy-start(s32[8]{0:T(128)} %constant.343.clone) | copy-start | bytes 100
  161.3 55.9 %all-to-all-start.1 = ((bf16[16,256,256]{2,0,1:T(8,128)(2,1)}), bf16[16,256,256]{2,0,1:T(8,128)(2,1)}, u32[]{:S(2)}, u32[]{:S(2)}) async-start(bf16[16,256,256]{2,0,1:T(8,128)(2,1)} %copy.40), calls=%async_computation.1 | async-start | bytes 4194304 | tf_op jit(solution)/shard_map/all_to_all | solution.py:104
  217.1 2.8 copy-start.5
  237.4 37.0 %all-to-all-start.2 = ((bf16[64,64,256]{2,0,1:T(8,128)(2,1)}), bf16[64,64,256]{2,0,1:T(8,128)(2,1)}, u32[]{:S(2)}, u32[]{:S(2)}) async-start(bf16[64,64,256]{2,0,1:T(8,128)(2,1)} %copy.44), calls=%async_computation.2 | async-start | bytes 4194304 | tf_op jit(solution)/shard_map/all_to_all | solution.py:114
  242.8 5.9 %collective-permute-start.28 = (f32[4,64,64]{2,1,0:T(8,128)S(1)}, f32[4,64,64]{2,1,0:T(8,128)S(1)}, u32[]{:S(2)}, u32[]{:S(2)}) collective-permute-start(f32[4,64,64]{2,1,0:T(8,128)S(1)} %dynamic-slice_bitcast_fusion.2), channel_id=1, source_target_pairs={{0,8},{4,0},{12,4},{20,12},{28,20},{24,28},{16,24},{8,16},{1,9},{5... | collective-permute-start | bytes 196616 | tf_op jit(solution)/shard_map/ppermute | solution.py:72
  242.9 7.1 %collective-permute-start.21 = (f32[4,64,64]{2,1,0:T(8,128)S(1)}, f32[4,64,64]{2,1,0:T(8,128)S(1)}, u32[]{:S(2)}, u32[]{:S(2)}) collective-permute-start(f32[4,64,64]{2,1,0:T(8,128)S(1)} %dynamic-slice_bitcast_fusion.3), channel_id=1, source_target_pairs={{0,4},{4,12},{12,20},{20,28},{28,24},{24,16},{16,8},{8,0},{1,5},{5... | collective-permute-start | bytes 196616 | tf_op jit(solution)/shard_map/ppermute | solution.py:72
  249.6 5.2 %collective-permute-start.29 = (f32[4,64,64]{2,1,0:T(8,128)S(1)}, f32[4,64,64]{2,1,0:T(8,128)S(1)}, u32[]{:S(2)}, u32[]{:S(2)}) collective-permute-start(f32[4,64,64]{2,1,0:T(8,128)S(1)} %bitcast_add_fusion.20), channel_id=1, source_target_pairs={{0,8},{4,0},{12,4},{20,12},{28,20},{24,28},{16,24},{8,16},{1,9},{5... | collective-permute-start | bytes 196616 | tf_op jit(solution)/shard_map/ppermute | solution.py:72
  250.0 6.3 %collective-permute-start.22 = (f32[4,64,64]{2,1,0:T(8,128)S(1)}, f32[4,64,64]{2,1,0:T(8,128)S(1)}, u32[]{:S(2)}, u32[]{:S(2)}) collective-permute-start(f32[4,64,64]{2,1,0:T(8,128)S(1)} %bitcast_add_fusion.27), channel_id=1, source_target_pairs={{0,4},{4,12},{12,20},{20,28},{28,24},{24,16},{16,8},{8,0},{1,5},{5... | collective-permute-start | bytes 196616 | tf_op jit(solution)/shard_map/ppermute | solution.py:72
  255.8 5.0 %collective-permute-start.30 = (f32[4,64,64]{2,1,0:T(8,128)S(1)}, f32[4,64,64]{2,1,0:T(8,128)S(1)}, u32[]{:S(2)}, u32[]{:S(2)}) collective-permute-start(f32[4,64,64]{2,1,0:T(8,128)S(1)} %bitcast_add_fusion.19), channel_id=1, source_target_pairs={{0,8},{4,0},{12,4},{20,12},{28,20},{24,28},{16,24},{8,16},{1,9},{5... | collective-permute-start | bytes 196616 | tf_op jit(solution)/shard_map/ppermute | solution.py:72
  256.4 5.9 %collective-permute-start.23 = (f32[4,64,64]{2,1,0:T(8,128)S(1)}, f32[4,64,64]{2,1,0:T(8,128)S(1)}, u32[]{:S(2)}, u32[]{:S(2)}) collective-permute-start(f32[4,64,64]{2,1,0:T(8,128)S(1)} %bitcast_add_fusion.26), channel_id=1, source_target_pairs={{0,4},{4,12},{12,20},{20,28},{28,24},{24,16},{16,8},{8,0},{1,5},{5... | collective-permute-start | bytes 196616 | tf_op jit(solution)/shard_map/ppermute | solution.py:72
  261.7 5.0 %collective-permute-start.31 = (f32[4,64,64]{2,1,0:T(8,128)S(1)}, f32[4,64,64]{2,1,0:T(8,128)S(1)}, u32[]{:S(2)}, u32[]{:S(2)}) collective-permute-start(f32[4,64,64]{2,1,0:T(8,128)S(1)} %bitcast_add_fusion.18), channel_id=1, source_target_pairs={{0,8},{4,0},{12,4},{20,12},{28,20},{24,28},{16,24},{8,16},{1,9},{5... | collective-permute-start | bytes 196616 | tf_op jit(solution)/shard_map/ppermute | solution.py:72
  262.3 5.9 %collective-permute-start.24 = (f32[4,64,64]{2,1,0:T(8,128)S(1)}, f32[4,64,64]{2,1,0:T(8,128)S(1)}, u32[]{:S(2)}, u32[]{:S(2)}) collective-permute-start(f32[4,64,64]{2,1,0:T(8,128)S(1)} %bitcast_add_fusion.25), channel_id=1, source_target_pairs={{0,4},{4,12},{12,20},{20,28},{28,24},{24,16},{16,8},{8,0},{1,5},{5... | collective-permute-start | bytes 196616 | tf_op jit(solution)/shard_map/ppermute | solution.py:72
  267.7 5.1 %collective-permute-start.32 = (f32[4,64,64]{2,1,0:T(8,128)S(1)}, f32[4,64,64]{2,1,0:T(8,128)S(1)}, u32[]{:S(2)}, u32[]{:S(2)}) collective-permute-start(f32[4,64,64]{2,1,0:T(8,128)S(1)} %bitcast_add_fusion.17), channel_id=1, source_target_pairs={{0,8},{4,0},{12,4},{20,12},{28,20},{24,28},{16,24},{8,16},{1,9},{5... | collective-permute-start | bytes 196616 | tf_op jit(solution)/shard_map/ppermute | solution.py:72
  268.2 12.2 %collective-permute-start.25 = (f32[4,64,64]{2,1,0:T(8,128)S(1)}, f32[4,64,64]{2,1,0:T(8,128)}, u32[]{:S(2)}, u32[]{:S(2)}) collective-permute-start(f32[4,64,64]{2,1,0:T(8,128)S(1)} %bitcast_add_fusion.24), channel_id=1, source_target_pairs={{0,4},{4,12},{12,20},{20,28},{28,24},{24,16},{16,8},{8,0},{1,5},{5... | collective-permute-start | bytes 196616 | tf_op jit(solution)/shard_map/ppermute | solution.py:72
  273.7 15.1 %collective-permute-start.33 = (f32[4,64,64]{2,1,0:T(8,128)S(1)}, f32[4,64,64]{2,1,0:T(8,128)S(1)}, u32[]{:S(2)}, u32[]{:S(2)}) collective-permute-start(f32[4,64,64]{2,1,0:T(8,128)S(1)} %bitcast_add_fusion.16), channel_id=1, source_target_pairs={{0,8},{4,0},{12,4},{20,12},{28,20},{24,28},{16,24},{8,16},{1,9},{5... | collective-permute-start | bytes 196616 | tf_op jit(solution)/shard_map/ppermute | solution.py:72
  276.2 1.3 copy-start.2
  278.2 40.8 %copy-start.4 = (f32[8,16,16,256]{3,1,0,2:T(8,128)}, f32[8,16,16,256]{3,1,0,2:T(8,128)S(1)}, u32[]{:S(2)}) copy-start(f32[8,16,16,256]{3,1,0,2:T(8,128)S(1)} %get-tuple-element.4) | copy-start | bytes 6291460
  278.2 41.9 %copy-start.3 = (f32[8,16,16,256]{3,1,0,2:T(8,128)}, f32[8,16,16,256]{3,1,0,2:T(8,128)S(1)}, u32[]{:S(2)}) copy-start(f32[8,16,16,256]{3,1,0,2:T(8,128)S(1)} %get-tuple-element.3) | copy-start | bytes 6291460
  278.3 7.7 %collective-permute-start.14 = (f32[16,16,256]{2,0,1:T(8,128)S(1)}, f32[16,16,256]{2,0,1:T(8,128)S(1)}, u32[]{:S(2)}, u32[]{:S(2)}) collective-permute-start(f32[16,16,256]{2,0,1:T(8,128)S(1)} %dynamic-slice_bitcast_fusion), channel_id=1, source_target_pairs={{0,8},{4,0},{12,4},{20,12},{28,20},{24,28},{16,24},{8,16},{1,9},{5... | collective-permute-start | bytes 786440 | tf_op jit(solution)/shard_map/ppermute | solution.py:72
  278.6 8.0 %collective-permute-start.7 = (f32[16,16,256]{2,0,1:T(8,128)S(1)}, f32[16,16,256]{2,0,1:T(8,128)S(1)}, u32[]{:S(2)}, u32[]{:S(2)}) collective-permute-start(f32[16,16,256]{2,0,1:T(8,128)S(1)} %dynamic-slice_bitcast_fusion.1), channel_id=1, source_target_pairs={{0,4},{4,12},{12,20},{20,28},{28,24},{24,16},{16,8},{8,0},{1,5},{5... | collective-permute-start | bytes 786440 | tf_op jit(solution)/shard_map/ppermute | solution.py:72
  281.3 16.6 %collective-permute-start.26 = (f32[4,64,64]{2,1,0:T(8,128)S(1)}, f32[4,64,64]{2,1,0:T(8,128)S(1)}, u32[]{:S(2)}, u32[]{:S(2)}) collective-permute-start(f32[4,64,64]{2,1,0:T(8,128)S(1)} %bitcast_add_fusion.23), channel_id=1, source_target_pairs={{0,4},{4,12},{12,20},{20,28},{28,24},{24,16},{16,8},{8,0},{1,5},{5... | collective-permute-start | bytes 196616 | tf_op jit(solution)/shard_map/ppermute | solution.py:72
  286.0 9.7 %collective-permute-start.15 = (f32[16,16,256]{2,0,1:T(8,128)S(1)}, f32[16,16,256]{2,0,1:T(8,128)S(1)}, u32[]{:S(2)}, u32[]{:S(2)}) collective-permute-start(f32[16,16,256]{2,0,1:T(8,128)S(1)} %bitcast_add_fusion.6), channel_id=1, source_target_pairs={{0,8},{4,0},{12,4},{20,12},{28,20},{24,28},{16,24},{8,16},{1,9},{5... | collective-permute-start | bytes 786440 | tf_op jit(solution)/shard_map/ppermute | solution.py:72
  286.7 9.1 %collective-permute-start.8 = (f32[16,16,256]{2,0,1:T(8,128)S(1)}, f32[16,16,256]{2,0,1:T(8,128)S(1)}, u32[]{:S(2)}, u32[]{:S(2)}) collective-permute-start(f32[16,16,256]{2,0,1:T(8,128)S(1)} %bitcast_add_fusion.13), channel_id=1, source_target_pairs={{0,4},{4,12},{12,20},{20,28},{28,24},{24,16},{16,8},{8,0},{1,5},{5... | collective-permute-start | bytes 786440 | tf_op jit(solution)/shard_map/ppermute | solution.py:72
  289.7 16.8 %collective-permute-start.34 = (f32[4,64,64]{2,1,0:T(8,128)S(1)}, f32[4,64,64]{2,1,0:T(8,128)S(1)}, u32[]{:S(2)}, u32[]{:S(2)}) collective-permute-start(f32[4,64,64]{2,1,0:T(8,128)S(1)} %bitcast_add_fusion.15), channel_id=1, source_target_pairs={{0,8},{4,0},{12,4},{20,12},{28,20},{24,28},{16,24},{8,16},{1,9},{5... | collective-permute-start | bytes 196616 | tf_op jit(solution)/shard_map/ppermute | solution.py:72
  295.8 8.6 %collective-permute-start.16 = (f32[16,16,256]{2,0,1:T(8,128)S(1)}, f32[16,16,256]{2,0,1:T(8,128)S(1)}, u32[]{:S(2)}, u32[]{:S(2)}) collective-permute-start(f32[16,16,256]{2,0,1:T(8,128)S(1)} %bitcast_add_fusion.5), channel_id=1, source_target_pairs={{0,8},{4,0},{12,4},{20,12},{28,20},{24,28},{16,24},{8,16},{1,9},{5... | collective-permute-start | bytes 786440 | tf_op jit(solution)/shard_map/ppermute | solution.py:72
  295.9 8.8 %collective-permute-start.9 = (f32[16,16,256]{2,0,1:T(8,128)S(1)}, f32[16,16,256]{2,0,1:T(8,128)S(1)}, u32[]{:S(2)}, u32[]{:S(2)}) collective-permute-start(f32[16,16,256]{2,0,1:T(8,128)S(1)} %bitcast_add_fusion.12), channel_id=1, source_target_pairs={{0,4},{4,12},{12,20},{20,28},{28,24},{24,16},{16,8},{8,0},{1,5},{5... | collective-permute-start | bytes 786440 | tf_op jit(solution)/shard_map/ppermute | solution.py:72
  298.0 16.4 %collective-permute-start.27 = (f32[4,64,64]{2,1,0:T(8,128)S(1)}, f32[4,64,64]{2,1,0:T(8,128)S(1)}, u32[]{:S(2)}, u32[]{:S(2)}) collective-permute-start(f32[4,64,64]{2,1,0:T(8,128)S(1)} %bitcast_add_fusion.22), channel_id=1, source_target_pairs={{0,4},{4,12},{12,20},{20,28},{28,24},{24,16},{16,8},{8,0},{1,5},{5... | collective-permute-start | bytes 196616 | tf_op jit(solution)/shard_map/ppermute | solution.py:72
  304.4 7.8 %collective-permute-start.17 = (f32[16,16,256]{2,0,1:T(8,128)S(1)}, f32[16,16,256]{2,0,1:T(8,128)S(1)}, u32[]{:S(2)}, u32[]{:S(2)}) collective-permute-start(f32[16,16,256]{2,0,1:T(8,128)S(1)} %bitcast_add_fusion.4), channel_id=1, source_target_pairs={{0,8},{4,0},{12,4},{20,12},{28,20},{24,28},{16,24},{8,16},{1,9},{5... | collective-permute-start | bytes 786440 | tf_op jit(solution)/shard_map/ppermute | solution.py:72
  304.8 8.1 %collective-permute-start.10 = (f32[16,16,256]{2,0,1:T(8,128)S(1)}, f32[16,16,256]{2,0,1:T(8,128)S(1)}, u32[]{:S(2)}, u32[]{:S(2)}) collective-permute-start(f32[16,16,256]{2,0,1:T(8,128)S(1)} %bitcast_add_fusion.11), channel_id=1, source_target_pairs={{0,4},{4,12},{12,20},{20,28},{28,24},{24,16},{16,8},{8,0},{1,5},{5... | collective-permute-start | bytes 786440 | tf_op jit(solution)/shard_map/ppermute | solution.py:72
  312.2 6.9 %collective-permute-start.18 = (f32[16,16,256]{2,0,1:T(8,128)S(1)}, f32[16,16,256]{2,0,1:T(8,128)S(1)}, u32[]{:S(2)}, u32[]{:S(2)}) collective-permute-start(f32[16,16,256]{2,0,1:T(8,128)S(1)} %bitcast_add_fusion.3), channel_id=1, source_target_pairs={{0,8},{4,0},{12,4},{20,12},{28,20},{24,28},{16,24},{8,16},{1,9},{5... | collective-permute-start | bytes 786440 | tf_op jit(solution)/shard_map/ppermute | solution.py:72
  312.9 7.2 %collective-permute-start.11 = (f32[16,16,256]{2,0,1:T(8,128)S(1)}, f32[16,16,256]{2,0,1:T(8,128)S(1)}, u32[]{:S(2)}, u32[]{:S(2)}) collective-permute-start(f32[16,16,256]{2,0,1:T(8,128)S(1)} %bitcast_add_fusion.10), channel_id=1, source_target_pairs={{0,4},{4,12},{12,20},{20,28},{28,24},{24,16},{16,8},{8,0},{1,5},{5... | collective-permute-start | bytes 786440 | tf_op jit(solution)/shard_map/ppermute | solution.py:72
  319.1 6.9 %collective-permute-start.19 = (f32[16,16,256]{2,0,1:T(8,128)S(1)}, f32[16,16,256]{2,0,1:T(8,128)S(1)}, u32[]{:S(2)}, u32[]{:S(2)}) collective-permute-start(f32[16,16,256]{2,0,1:T(8,128)S(1)} %bitcast_add_fusion.2), channel_id=1, source_target_pairs={{0,8},{4,0},{12,4},{20,12},{28,20},{24,28},{16,24},{8,16},{1,9},{5... | collective-permute-start | bytes 786440 | tf_op jit(solution)/shard_map/ppermute | solution.py:72
  320.2 8.2 %collective-permute-start.12 = (f32[16,16,256]{2,0,1:T(8,128)S(1)}, f32[16,16,256]{2,0,1:T(8,128)S(1)}, u32[]{:S(2)}, u32[]{:S(2)}) collective-permute-start(f32[16,16,256]{2,0,1:T(8,128)S(1)} %bitcast_add_fusion.9), channel_id=1, source_target_pairs={{0,4},{4,12},{12,20},{20,28},{28,24},{24,16},{16,8},{8,0},{1,5},{5... | collective-permute-start | bytes 786440 | tf_op jit(solution)/shard_map/ppermute | solution.py:72
  327.0 8.0 %collective-permute-start.20 = (f32[16,16,256]{2,0,1:T(8,128)S(1)}, f32[16,16,256]{2,0,1:T(8,128)S(1)}, u32[]{:S(2)}, u32[]{:S(2)}) collective-permute-start(f32[16,16,256]{2,0,1:T(8,128)S(1)} %bitcast_add_fusion.1), channel_id=1, source_target_pairs={{0,8},{4,0},{12,4},{20,12},{28,20},{24,28},{16,24},{8,16},{1,9},{5... | collective-permute-start | bytes 786440 | tf_op jit(solution)/shard_map/ppermute | solution.py:72
  329.3 6.6 %collective-permute-start.13 = (f32[16,16,256]{2,0,1:T(8,128)S(1)}, f32[16,16,256]{2,0,1:T(8,128)S(1)}, u32[]{:S(2)}, u32[]{:S(2)}) collective-permute-start(f32[16,16,256]{2,0,1:T(8,128)S(1)} %bitcast_add_fusion.8), channel_id=1, source_target_pairs={{0,4},{4,12},{12,20},{20,28},{28,24},{24,16},{16,8},{8,0},{1,5},{5... | collective-permute-start | bytes 786440 | tf_op jit(solution)/shard_map/ppermute | solution.py:72
